TPU v7x, 128 devices: a whole 4x4x4 slice. The times are simulated.
128 devices in a mesh: req: 4 (over y), head: 8 (over z, x_hi), blk: 4 (over x_lo, core).
Axes of the slice: x: 4 (x_hi: 2, x_lo: 2; x = x_hi * 2 + x_lo), y: 4, z: 4, core: 2. Of those that a mesh axis runs over, the one named last changes fastest.
Arguments:
- image_hidden: bfloat16 [16, 32, 32, 1536], P('req', 'head', 'blk'), parts along dimension 0, may hold values from -6 to 6
- text_hidden: bfloat16 [16, 160, 1536], P('req', ('head', 'blk')), parts along dimension 0, may hold values from -6 to 6
- latent_grid: float32 [16, 64, 64, 16], P('req', 'head', 'blk'), parts along dimension 0, may hold values from -6 to 6
- text_lengths: int32 [16], P('req'), parts along dimension 0, may hold values from 38 to 154, as said below
- step_index: int32 [16], P('req'), parts along dimension 0, may hold values from 125 to 999
- image_mod: float32 [16, 6, 1536], P('req'), parts along dimension 0, may hold values from -3 to 3
- text_mod: float32 [16, 6, 1536], P('req'), parts along dimension 0, may hold values from -3 to 3
- final_mod: float32 [16, 2, 1536], P('req'), parts along dimension 0, may hold values from -3 to 3
- image_qk_gain: float32 [2, 64], replicated, may hold values from 0.5 to 2.3
- text_qk_gain: float32 [2, 64], replicated, may hold values from 0.5 to 2.3
- image_qkv: bfloat16 [1536, 3, 1536], P(None, None, 'head'), may hold values from -0.15625 to 0.15625
- text_qkv: bfloat16 [1536, 3, 1536], P(None, None, 'head'), may hold values from -0.15625 to 0.15625
- image_proj: bfloat16 [1536, 1536], P('head'), may hold values from -0.15625 to 0.15625
- text_proj: bfloat16 [1536, 1536], P('head'), may hold values from -0.15625 to 0.15625
- image_up: bfloat16 [1536, 6144], P(None, 'head'), may hold values from -0.15625 to 0.15625
- text_up: bfloat16 [1536, 6144], P(None, 'head'), may hold values from -0.15625 to 0.15625
- image_down: bfloat16 [6144, 1536], P('head'), may hold values from -0.078125 to 0.078125
- text_down: bfloat16 [6144, 1536], P('head'), may hold values from -0.078125 to 0.078125
- final_proj: bfloat16 [1536, 64], replicated, may hold values from -0.15625 to 0.15625
- conv_kernel: bfloat16 [3, 3, 16, 512], replicated, may hold values from -0.5 to 0.5
Outputs:
- image_states: bfloat16 [16, 32, 32, 1536], P('req', 'head', 'blk'), parts along dimension 0
- text_states: bfloat16 [16, 160, 1536], P('req', ('head', 'blk')), parts along dimension 0
- latent_next: float32 [16, 64, 64, 16], P('req', 'head', 'blk'), parts along dimension 0
- features: bfloat16 [16, 64, 64, 512], P('req', 'head', 'blk'), parts along dimension 0
There are 4 independent parts, one for each index of `req`. A program takes and returns all parts, laid end to end along the dimension named above; an argument that names none is the same for every part. Nothing has to cross between parts.
Inputs may be any that keep to these rules, and one draw needn't show every extreme that they name: `text_lengths`: every request has 154 or fewer live text tokens, and in each group one request has exactly 154.
All inputs are finite; a program needn't handle non-finite values.
Results may differ from a plain program's by a relative error of at most 0.012.
Values may be sent and summed in bfloat16 or wider, within the bound.
No kernel may reach another device: no remote copies, remote signals or barrier semaphores. Data moves between devices by JAX's collectives and lax.ppermute only.
A program may use at most 128 MiB of HBM per device.

v0:
```python
import math
import jax
import jax.numpy as jnp
from jax import lax
from jax.sharding import PartitionSpec as P

HD = 64


def extended(block, sides, width):
    for axis, dim in sides:
        count = lax.axis_size(axis)
        forward = [(i, i + 1) for i in range(count - 1)]
        backward = [(target, source) for source, target in forward]
        low = lax.ppermute(
            lax.slice_in_dim(block, block.shape[dim] - width, None, axis=dim), axis, forward
        )
        high = lax.ppermute(lax.slice_in_dim(block, 0, width, axis=dim), axis, backward)
        block = jnp.concatenate([low, block, high], axis=dim)
    return block


def expand(vector, values):
    return vector.reshape((vector.shape[0],) + (1,) * (values.ndim - 2) + (vector.shape[-1],))


def modulate(values, shift, scale):
    average = jnp.mean(values, -1, keepdims=True)
    centred = values - average
    spread = jnp.mean(centred * centred, -1, keepdims=True)
    normed = centred * lax.rsqrt(spread + 1e-06)
    return normed * (1.0 + expand(scale, values)) + expand(shift, values)


def head_norm(values, gain):
    shaped = values.reshape(values.shape[:-1] + (values.shape[-1] // HD, HD))
    return (shaped * lax.rsqrt(jnp.mean(shaped * shaped, -1, keepdims=True) + 1e-06) * gain).astype(
        jnp.bfloat16
    )


def noise_level(fraction):
    return 3.0 * fraction / (1.0 + 2.0 * fraction)


def attention_inputs(normed, weight, gains):
    projected = jnp.einsum("rnd,dje->rnje", normed, weight, preferred_element_type=jnp.float32)
    queries = head_norm(projected[:, :, 0], gains[0])
    key_heads = head_norm(projected[:, :, 1], gains[1])
    value_heads = projected[:, :, 2].reshape(queries.shape).astype(jnp.bfloat16)
    return (queries, key_heads, value_heads)


def convolve(padded, kernel):
    out_rows = padded.shape[1] - 2
    out_cols = padded.shape[2] - 2
    summed = jnp.zeros((padded.shape[0], out_rows, out_cols, kernel.shape[-1]), jnp.float32)
    for row_off in range(3):
        for col_off in range(3):
            summed = summed + jnp.einsum(
                "rhwc,co->rhwo",
                padded[:, row_off : row_off + out_rows, col_off : col_off + out_cols],
                kernel[row_off, col_off],
                preferred_element_type=jnp.float32,
            )
    return summed.astype(jnp.bfloat16)


def body(
    image_hidden,
    text_hidden,
    latent_grid,
    text_lengths,
    step_index,
    image_mod,
    text_mod,
    final_mod,
    image_qk_gain,
    text_qk_gain,
    image_qkv,
    text_qkv,
    image_proj,
    text_proj,
    image_up,
    text_up,
    image_down,
    text_down,
    final_proj,
    conv_kernel,
):
    blocks = lax.axis_size("blk")
    requests, tile_rows, tile_cols, model_width = image_hidden.shape
    text_slice = text_hidden.shape[1]
    image_full, text_full = (
        lax.all_gather(image_hidden, "head", axis=1, tiled=True),
        lax.all_gather(text_hidden, "head", axis=1, tiled=True),
    )
    grid_rows = image_full.shape[1]
    image_rows = grid_rows * tile_cols
    text_rows = text_full.shape[1]
    local_rows = image_rows + text_rows
    image_flat = image_full.reshape(requests, image_rows, model_width).astype(jnp.float32)
    text_flat = text_full.astype(jnp.float32)
    image_norm = modulate(image_flat, image_mod[:, 0], image_mod[:, 1]).astype(jnp.bfloat16)
    text_norm = modulate(text_flat, text_mod[:, 0], text_mod[:, 1]).astype(jnp.bfloat16)
    image_q, image_k, image_v = attention_inputs(image_norm, image_qkv, image_qk_gain)
    text_q, text_k, text_v = attention_inputs(text_norm, text_qkv, text_qk_gain)
    queries = jnp.concatenate([image_q, text_q], 1)
    key_heads = jnp.concatenate([image_k, text_k], 1)
    value_heads = jnp.concatenate([image_v, text_v], 1)
    local_heads = queries.shape[2]
    score_scale = 1.0 / math.sqrt(HD)
    key_piece = lax.all_gather(key_heads, "blk", axis=1, tiled=True)
    value_piece = lax.all_gather(value_heads, "blk", axis=1, tiled=True)
    span_rows = key_piece.shape[1]
    position = jnp.arange(span_rows, dtype=jnp.int32)
    source = position // local_rows
    within = position % local_rows
    text_pos = within - image_rows
    owner = text_pos // text_slice
    slot_ids = (owner * blocks + source) * text_slice + text_pos % text_slice
    usable = (within < image_rows)[None, :] | (slot_ids[None, :] < text_lengths[:, None])
    scores = (
        jnp.einsum("rqhd,rkhd->rhqk", queries, key_piece, preferred_element_type=jnp.float32)
        * score_scale
    )
    weights = jnp.exp(scores) * usable[:, None, None, :].astype(jnp.float32)
    denominator = jnp.sum(weights, -1)
    numerator = jnp.einsum(
        "rhqk,rkhd->rhqd",
        weights.astype(jnp.bfloat16),
        value_piece,
        preferred_element_type=jnp.float32,
    )
    numerator, denominator = (numerator, denominator)
    context = (numerator / denominator[..., None]).astype(jnp.bfloat16)
    local_width = local_heads * HD
    context = context.transpose(0, 2, 1, 3).reshape(requests, local_rows, local_width)
    image_part = jnp.einsum(
        "rne,ed->rnd", context[:, :image_rows], image_proj, preferred_element_type=jnp.float32
    )
    text_part = jnp.einsum(
        "rne,ed->rnd", context[:, image_rows:], text_proj, preferred_element_type=jnp.float32
    )
    image_attn, text_attn = (
        lax.psum_scatter(
            image_part.reshape(requests, grid_rows, tile_cols, model_width).astype(jnp.bfloat16),
            "head",
            scatter_dimension=1,
            tiled=True,
        ).astype(jnp.float32),
        lax.psum_scatter(
            text_part.astype(jnp.bfloat16), "head", scatter_dimension=1, tiled=True
        ).astype(jnp.float32),
    )
    image_mid = image_hidden.astype(jnp.float32) + expand(image_mod[:, 2], image_attn) * image_attn
    text_mid = text_hidden.astype(jnp.float32) + expand(text_mod[:, 2], text_attn) * text_attn
    image_local = modulate(image_mid, image_mod[:, 3], image_mod[:, 4]).astype(jnp.bfloat16)
    text_local = modulate(text_mid, text_mod[:, 3], text_mod[:, 4]).astype(jnp.bfloat16)
    image_in, text_in = (
        lax.all_gather(image_local, "head", axis=1, tiled=True),
        lax.all_gather(text_local, "head", axis=1, tiled=True),
    )
    image_in = image_in.reshape(requests, image_rows, model_width)
    image_hid = jax.nn.gelu(
        jnp.einsum("rnd,df->rnf", image_in, image_up, preferred_element_type=jnp.float32),
        approximate=True,
    ).astype(jnp.bfloat16)
    text_hid = jax.nn.gelu(
        jnp.einsum("rnd,df->rnf", text_in, text_up, preferred_element_type=jnp.float32),
        approximate=True,
    ).astype(jnp.bfloat16)
    image_back = jnp.einsum(
        "rnf,fd->rnd", image_hid, image_down, preferred_element_type=jnp.float32
    ).reshape(requests, grid_rows, tile_cols, model_width)
    text_back = jnp.einsum("rnf,fd->rnd", text_hid, text_down, preferred_element_type=jnp.float32)
    image_mlp, text_mlp = (
        lax.psum_scatter(
            image_back.astype(jnp.bfloat16), "head", scatter_dimension=1, tiled=True
        ).astype(jnp.float32),
        lax.psum_scatter(
            text_back.astype(jnp.bfloat16), "head", scatter_dimension=1, tiled=True
        ).astype(jnp.float32),
    )
    image_out = image_mid + expand(image_mod[:, 5], image_mlp) * image_mlp
    image_states = image_out.astype(jnp.bfloat16)
    text_states = (text_mid + expand(text_mod[:, 5], text_mlp) * text_mlp).astype(jnp.bfloat16)
    final_in = modulate(image_out, final_mod[:, 1], final_mod[:, 0]).astype(jnp.bfloat16)
    velocity = jnp.einsum("rhwd,dp->rhwp", final_in, final_proj, preferred_element_type=jnp.float32)
    channels = velocity.shape[-1] // 4
    velocity = (
        velocity.reshape(requests, tile_rows, tile_cols, 2, 2, channels)
        .transpose(0, 1, 3, 2, 4, 5)
        .reshape(requests, 2 * tile_rows, 2 * tile_cols, channels)
    )
    current = step_index.astype(jnp.float32) / 1000.0
    following = jnp.maximum(step_index - 125, 0).astype(jnp.float32) / 1000.0
    step_size = noise_level(following) - noise_level(current)
    latent_next = latent_grid + step_size[:, None, None, None] * velocity
    decoded_in = (latent_next / 1.5305 + 0.0609).astype(jnp.bfloat16)
    padded = extended(decoded_in, (("head", 1), ("blk", 2)), 1)
    features = convolve(padded, conv_kernel)
    return (image_states, text_states, latent_next, features)


def solution(mesh):
    in_specs = (
        P("req", "head", "blk", None),
        P("req", ("head", "blk"), None),
        P("req", "head", "blk", None),
        P("req"),
        P("req"),
        P("req", None, None),
        P("req", None, None),
        P("req", None, None),
        P(),
        P(),
        P(None, None, "head"),
        P(None, None, "head"),
        P("head", None),
        P("head", None),
        P(None, "head"),
        P(None, "head"),
        P("head", None),
        P("head", None),
        P(),
        P(),
    )
    out_specs = (
        P("req", "head", "blk", None),
        P("req", ("head", "blk"), None),
        P("req", "head", "blk", None),
        P("req", "head", "blk", None),
    )
    return jax.shard_map(body, mesh=mesh, in_specs=in_specs, out_specs=out_specs, check_vma=False)
```

profile of v0, /device:TPU:1, one launch (start us, length us, event | category | flops | bytes accessed | tf_op | source)
XLA Modules:
  0.0 633.5 jit_solution(10010168062454504127)
XLA Ops:
  11.7 33.0 %all_gather.19 = bf16[4,40,1536]{2,0,1:T(4,128)(2,1)S(1)} all-gather(bf16[4,5,1536]{2,0,1:T(4,128)(2,1)} %param.21), channel_id=1, replica_groups=mesh['req'=4,'head'=8,'blk'=4] {'head'}, dimensions={1}, use_global_device_ids=true | all-gather | bytes 552960 | tf_op jit(solution)/shard_map/all_gather | solution.py:96
  49.0 28.9 %all-gather.5.cloned.1.call-done = bf16[4,32,8,1536]{3,2,1,0:T(8,128)(2,1)} async-done(((bf16[4,4,8,1536]{3,2,1,0:T(8,128)(2,1)}), bf16[4,32,8,1536]{3,2,1,0:T(8,128)(2,1)}) %all-gather.5.cloned.1.call-update) | async-done | bytes 3145744 | tf_op jit(solution)/shard_map/all_gather | solution.py:95
  77.8 2.4 convert_reduce_fusion
  80.3 2.9 fusion.11
  83.3 4.6 fusion.25
  90.3 3.1 copy.76
  102.3 2.1 copy.78
  104.4 2.9 pad_maximum_fusion
  112.4 21.7 %all-gather.7.cloned.1.call-done = bf16[4,1184,3,64]{3,0,2,1:T(4,128)(2,1)} async-done(((bf16[4,296,3,64]{3,0,2,1:T(4,128)(2,1)}), bf16[4,1184,3,64]{3,0,2,1:T(4,128)(2,1)}) %all-gather.7.cloned.1.call-update) | async-done | bytes 1818640 | tf_op jit(solution)/shard_map/all_gather | solution.py:113
  134.1 10.5 %fusion = (f32[4,3,296]{2,1,0:T(4,128)S(1)}, f32[4,3,296,1184]{3,2,1,0:T(8,128)}) fusion(f32[4,1184]{1,0:T(4,128)S(1)} %or_convert_fusion, bf16[4,1184,3,64]{3,0,2,1:T(4,128)(2,1)} %all-gather.7.cloned.1.call-done, bf16[4,40,3,64]{1,3,2,0:T(8,128)(2,1)S(1)} %multiply_convert_fusion.3, bf16[4,256,3,64]{1,3,2,0:T(8,128)(2,1)} %multiply_convert_fusion.1), kind=kOutput, calls=%fused_computation.2 | convolution fusion | flops 551835136 | bytes 19128704 | tf_op jit(solution)/shard_map/rqhd,rkhd->rhqk/dot_general | solution.py:124
  144.6 34.0 %all-gather.9.cloned.1.call-done = bf16[4,1184,3,64]{3,0,2,1:T(4,128)(2,1)} async-done(((bf16[4,296,3,64]{3,0,2,1:T(4,128)(2,1)}), bf16[4,1184,3,64]{3,0,2,1:T(4,128)(2,1)}) %all-gather.9.cloned.1.call-update) | async-done | bytes 1818640 | tf_op jit(solution)/shard_map/all_gather | solution.py:114
  178.5 9.1 %divide_convert_fusion = bf16[4,296,3,64]{1,3,2,0:T(8,128)(2,1)S(1)} fusion(bf16[4,1184,3,64]{3,0,2,1:T(4,128)(2,1)} %all-gather.9.cloned.1.call-done, f32[4,3,296,1184]{3,2,1,0:T(8,128)} %get-tuple-element.49, f32[4,1184]{1,0:T(4,128)S(1)} %or_convert_fusion, f32[4,296,3]{1,2,0:T(4,128)S(1)} %bitcast.223), kind=kOutput, calls=%fused_computation.61 | convolution fusion | flops 547178496 | bytes 19128704 | tf_op jit(solution)/shard_map/rhqk,rkhd->rhqd/dot_general | solution.py:129
  187.6 2.7 fusion.15
  193.2 164.2 %all-reduce.11.cloned.1.call-done = (bf16[4,32,8,1536]{3,2,1,0:T(8,128)(2,1)}, bf16[4,40,1536]{2,0,1:T(4,128)(2,1)}) async-done(((bf16[4,32,8,1536]{3,2,1,0:T(8,128)(2,1)}, bf16[4,40,1536]{2,0,1:T(4,128)(2,1)}), (bf16[4,32,8,1536]{3,2,1,0:T(8,128)(2,1)}, bf16[4,40,1536]{2,0,1:T(4,128)(2,1)})) %all-reduce.11.cloned.1.call-update) | async-done | bytes 3637264
  365.7 30.7 %all_gather.23 = bf16[4,40,1536]{2,0,1:T(4,128)(2,1)S(1)} all-gather(bf16[4,5,1536]{2,0,1:T(4,128)(2,1)S(1)} %add_convert_fusion.5), channel_id=1, replica_groups=mesh['req'=4,'head'=8,'blk'=4] {'head'}, dimensions={1}, use_global_device_ids=true | all-gather | bytes 552960 | tf_op jit(solution)/shard_map/all_gather | solution.py:162
  396.4 4.8 convolution_convert_fusion.2
  401.2 2.1 copy.86
  403.3 23.0 %all-gather.11.cloned.1.call-done = bf16[4,32,8,1536]{3,2,1,0:T(8,128)(2,1)} async-done(((bf16[4,4,8,1536]{3,2,1,0:T(8,128)(2,1)}), bf16[4,32,8,1536]{3,2,1,0:T(8,128)(2,1)}) %all-gather.11.cloned.1.call-update) | async-done | bytes 3145744 | tf_op jit(solution)/shard_map/all_gather | solution.py:161
  426.2 10.5 %fusion.14 = bf16[4,32,8,1536]{3,2,1,0:T(8,128)(2,1)} fusion(bf16[768,1536]{1,0:T(8,128)(2,1)S(1)} %copy-done, bf16[1536,768]{1,0:T(8,128)(2,1)} %param.34, bf16[4,32,8,1536]{3,2,1,0:T(8,128)(2,1)} %all-gather.11.cloned.1.call-done), kind=kOutput, calls=%fused_computation.21 | convolution fusion | flops 4840488960 | bytes 11010048 | tf_op jit(solution)/shard_map/rnf,fd->rnd/dot_general | solution.py:173
  437.6 161.8 %all-reduce.9.cloned.1.call-done = (bf16[4,32,8,1536]{3,2,1,0:T(8,128)(2,1)}, bf16[4,40,1536]{2,0,1:T(4,128)(2,1)}) async-done(((bf16[4,32,8,1536]{3,2,1,0:T(8,128)(2,1)}, bf16[4,40,1536]{2,0,1:T(4,128)(2,1)}), (bf16[4,32,8,1536]{3,2,1,0:T(8,128)(2,1)}, bf16[4,40,1536]{2,0,1:T(4,128)(2,1)})) %all-reduce.9.cloned.1.call-update) | async-done | bytes 3637264
  600.8 2.2 multiply_reduce_fusion
  610.9 2.8 collective-permute-done.1
  613.8 5.1 collective-permute-start.2
  621.4 2.6 collective-permute-done.3
  (147 shorter events, 50.0 us)
Async XLA Ops:
  7.2 419.1 %copy-start = (bf16[768,1536]{1,0:T(8,128)(2,1)S(1)}, bf16[768,1536]{1,0:T(8,128)(2,1)}, u32[]{:S(2)}) copy-start(bf16[768,1536]{1,0:T(8,128)(2,1)} %param.36) | copy-start | bytes 7077892
  7.2 70.7 %all-gather.5.cloned.1.call-start = ((), (), s32[]{:S(2)}) async-start(), calls=%async_computation | async-start | bytes 3538944 | tf_op jit(solution)/shard_map/all_gather | solution.py:95
  7.9 126.1 %all-gather.7.cloned.1.call-start = ((), (), s32[]{:S(2)}) async-start(), calls=%async_computation.1 | async-start | bytes 4546560 | tf_op jit(solution)/shard_map/all_gather | solution.py:113
  8.0 38.0 %copy-start.2 = (bf16[1536,3,192]{0,2,1:T(8,128)(2,1)S(1)}, bf16[1536,3,192]{0,2,1:T(8,128)(2,1)}, u32[]{:S(2)}) copy-start(bf16[1536,3,192]{0,2,1:T(8,128)(2,1)} %param.31) | copy-start | bytes 5308420
  45.4 2.8 copy-start.19
  48.9 34.4 %copy-start.16 = (f32[4,1536]{1,0:T(4,128)S(1)}, f32[4,1536]{1,0:T(4,128)}, u32[]{:S(2)}) copy-start(f32[4,1536]{1,0:T(4,128)} %get-tuple-element.36) | copy-start | bytes 73732
  48.9 34.4 %copy-start.17 = (f32[4,1,1536]{2,0,1:T(4,128)S(1)}, f32[4,1,1536]{2,0,1:T(4,128)}, u32[]{:S(2)}) copy-start(f32[4,1,1536]{2,0,1:T(4,128)} %copy.149) | copy-start | bytes 73732
  93.4 85.1 %all-gather.9.cloned.1.call-start = ((), (), s32[]{:S(2)}) async-start(), calls=%async_computation.2 | async-start | bytes 4546560 | tf_op jit(solution)/shard_map/all_gather | solution.py:114
  107.3 250.0 %all-reduce.11.cloned.1.call-start = ((), (), s32[]{:S(2)}) async-start(), calls=%async_computation.5 | async-start | bytes 7274496
  178.5 9.1 %copy-start.7 = (bf16[192,1536]{1,0:T(8,128)(2,1)S(1)}, bf16[192,1536]{1,0:T(8,128)(2,1)}, u32[]{:S(2)}) copy-start(bf16[192,1536]{1,0:T(8,128)(2,1)} %param.32) | copy-start | bytes 1769476
  190.4 167.0 %copy-start.1 = (bf16[4,4,8,1536]{3,2,1,0:T(8,128)(2,1)S(1)}, bf16[4,4,8,1536]{3,2,1,0:T(8,128)(2,1)}, u32[]{:S(2)}) copy-start(bf16[4,4,8,1536]{3,2,1,0:T(8,128)(2,1)} %param.20) | copy-start | bytes 1179652
  190.7 169.2 %copy-start.14 = (f32[4,1536]{1,0:T(4,128)S(1)}, f32[4,1536]{1,0:T(4,128)}, u32[]{:S(2)}) copy-start(f32[4,1536]{1,0:T(4,128)} %get-tuple-element.39) | copy-start | bytes 73732
  191.7 170.9 %copy-start.12 = (f32[4,1,1536]{2,0,1:T(4,128)S(1)}, f32[4,1,1536]{2,0,1:T(4,128)}, u32[]{:S(2)}) copy-start(f32[4,1,1536]{2,0,1:T(4,128)} %get-tuple-element.32) | copy-start | bytes 73732
  191.8 171.0 %copy-start.5 = (bf16[4,5,1536]{2,0,1:T(4,128)(2,1)S(1)}, bf16[4,5,1536]{2,0,1:T(4,128)(2,1)}, u32[]{:S(2)}) copy-start(bf16[4,5,1536]{2,0,1:T(4,128)(2,1)} %param.21) | copy-start | bytes 184324
  191.8 173.0 %copy-start.11 = (f32[4,1536]{1,0:T(4,128)S(1)}, f32[4,1536]{1,0:T(4,128)}, u32[]{:S(2)}) copy-start(f32[4,1536]{1,0:T(4,128)} %get-tuple-element.33) | copy-start | bytes 73732
  191.8 234.4 %all-gather.11.cloned.1.call-start = ((), (), s32[]{:S(2)}) async-start(), calls=%async_computation.3 | async-start | bytes 3538944 | tf_op jit(solution)/shard_map/all_gather | solution.py:161
  362.0 237.4 %all-reduce.9.cloned.1.call-start = ((), (), s32[]{:S(2)}) async-start(), calls=%async_computation.4 | async-start | bytes 7274496
  437.6 167.4 %copy-start.8 = (f32[4,8,16,16]{3,2,1,0:T(8,128)S(1)}, f32[4,8,16,16]{3,2,1,0:T(8,128)}, u32[]{:S(2)}) copy-start(f32[4,8,16,16]{3,2,1,0:T(8,128)} %param.22) | copy-start | bytes 98308
  600.8 8.3 %copy-start.10 = (f32[4,1536]{1,0:T(4,128)S(1)}, f32[4,1536]{1,0:T(4,128)}, u32[]{:S(2)}) copy-start(f32[4,1536]{1,0:T(4,128)} %get-tuple-element.28) | copy-start | bytes 73732
  600.8 9.9 %copy-start.9 = (bf16[3,3,16,512]{3,2,1,0:T(8,128)(2,1)S(1)}, bf16[3,3,16,512]{3,2,1,0:T(8,128)(2,1)}, u32[]{:S(2)}) copy-start(bf16[3,3,16,512]{3,2,1,0:T(8,128)(2,1)} %param.39) | copy-start | bytes 442372
  605.8 5.1 collective-permute-start
  607.8 6.0 collective-permute-start.1
  613.8 7.6 %collective-permute-start.2 = (bf16[4,10,1,16]{3,2,1,0:T(2,128)(2,1)S(1)}, bf16[4,10,1,16]{3,2,1,0:T(2,128)(2,1)S(1)}, u32[]{:S(2)}, u32[]{:S(2)}) collective-permute-start(bf16[4,10,1,16]{3,2,1,0:T(2,128)(2,1)S(1)} %get-tuple-element.26), channel_id=1, source_target_pairs={{0,1},{1,2},{2,3},{4,5},{5,6},{6,7},{8,9},{9,10},{10,11},{12,13},{... | collective-permute-start | bytes 3848 | tf_op jit(solution)/shard_map/ppermute | solution.py:15
  618.9 5.1 collective-permute-start.3
  (8 other events, 12.3 us)
Sparse Core Ops, SparseCore 0:
  10.3 67.4 all-gather.4
  93.5 40.4 all-gather.6
  135.7 42.7 all-gather.8
  191.9 165.4 all-reduce.10
  362.1 64.0 all-gather.10
  436.9 162.4 all-reduce.8
where the time goes:
time: 635 us; the launch traced here: 633 us
  waiting for transfers between devices  440 us (69%)
  blocking collectives  63.7 us (10%)
  matrix products  48.2 us (8%)
  other arithmetic  31.5 us (5%)
  local copies, waits for them, and re-layouts  23.8 us (4%)
  between operations  16 us (3%)
  starting transfers between devices  10.7 us (2%)
    unnamed x8, waiting for transfers between devices  327 us
    all_gather x1, waiting for transfers between devices, body(): value_piece = lax.all_gather(value_heads, 'blk', axis=1, tiled=True)  34 us
    all_gather x1, blocking collectives, body(): lax.all_gather(text_hidden, 'head', axis=1, tiled=True)  33 us
    all_gather x1, blocking collectives, body(): lax.all_gather(text_local, 'head', axis=1, tiled=True)  30.7 us
    all_gather x1, waiting for transfers between devices, body(): lax.all_gather(image_hidden, 'head', axis=1, tiled=True)  28.9 us
    all_gather x1, waiting for transfers between devices, body(): lax.all_gather(image_local, 'head', axis=1, tiled=True)  23 us
    all_gather x1, waiting for transfers between devices, body(): key_piece = lax.all_gather(key_heads, 'blk', axis=1, tiled=True)  21.7 us
  transfers between devices with their start and end apart: 10, of which 8 were waited for; matrix products, arithmetic and copies ran while one was open for 8% of the time, Pallas kernels for 0%

commit v1 on v0

--- a/solution.py
+++ b/solution.py
@@ -1,10 +1,23 @@
+import functools
 import math
 import jax
 import jax.numpy as jnp
 from jax import lax
 from jax.sharding import PartitionSpec as P
+from jax.lax import all_to_all, axis_size
 
 HD = 64
+
+
+def plan_stages_all_on_mesh(array_in, a_name):
+    upper = axis_size(a_name)
+    prior = jnp.stack(upper * [array_in], axis=0)
+    s_next = all_to_all(prior, a_name, split_axis=0, concat_axis=0)
+    r1 = jnp.concatenate(s_next, axis=1)
+    return r1
+
+
+fit_the_notes = functools.partial(plan_stages_all_on_mesh, a_name="head")
 
 
 def extended(block, sides, width):
@@ -92,7 +105,7 @@
     requests, tile_rows, tile_cols, model_width = image_hidden.shape
     text_slice = text_hidden.shape[1]
     image_full, text_full = (
-        lax.all_gather(image_hidden, "head", axis=1, tiled=True),
+        fit_the_notes(image_hidden),
         lax.all_gather(text_hidden, "head", axis=1, tiled=True),
     )
     grid_rows = image_full.shape[1]

time: 635 us -> 648 us (1.020)
  blocking collectives: 63.7 us -> 92.2 us
  waiting for transfers between devices: 440 us -> 416 us
  starting transfers between devices: 10.7 us -> 19.1 us
    all_gather x1 -> x0, waiting for transfers between devices: 28.9 us -> none  [body(): lax.all_gather(image_hidden, 'head', axis=1, tiled=True)]
    all_gather x1, blocking collectives: 33 us -> 61.5 us  [body(): lax.all_gather(text_hidden, 'head', axis=1, tiled=True)]
    all_to_all x0 -> x1, starting transfers between devices: none -> 8.45 us  [plan_stages_all_on_mesh(): s_next = all_to_all(prior, a_name, split_axis=0, concat_axis=0)]
    unnamed x8 -> x7, waiting for transfers between devices: 327 us -> 326 us
  transfers between devices with their start and end apart: 10 -> 10, of which waited for: 8 -> 7; matrix products, arithmetic and copies ran while one was open for 8% -> 7% of each run, Pallas kernels for 0% -> 0%
where the time goes in v1:
time: 648 us; the launch traced here: 647 us
  waiting for transfers between devices  416 us (64%)
  blocking collectives  92.2 us (14%)
  matrix products  45.5 us (7%)
  other arithmetic  32.1 us (5%)
  local copies, waits for them, and re-layouts  26.4 us (4%)
  starting transfers between devices  19.1 us (3%)
  between operations  15.7 us (2%)
    unnamed x7, waiting for transfers between devices  326 us
    all_gather x1, blocking collectives, body(): lax.all_gather(text_hidden, 'head', axis=1, tiled=True)  61.5 us
    all_gather x1, waiting for transfers between devices, body(): value_piece = lax.all_gather(value_heads, 'blk', axis=1, tiled=True)  34 us
    all_gather x1, blocking collectives, body(): lax.all_gather(text_local, 'head', axis=1, tiled=True)  30.7 us
    all_gather x1, waiting for transfers between devices, body(): key_piece = lax.all_gather(key_heads, 'blk', axis=1, tiled=True)  27.2 us
    all_gather x1, waiting for transfers between devices, body(): lax.all_gather(image_local, 'head', axis=1, tiled=True)  23 us
  transfers between devices with their start and end apart: 10, of which 7 were waited for; matrix products, arithmetic and copies ran while one was open for 7% of the time, Pallas kernels for 0%

profile of v1, /device:TPU:1, one launch (start us, length us, event | category | flops | bytes accessed | tf_op | source)
XLA Modules:
  0.0 646.8 jit_solution(9161280172609846253)
XLA Ops:
  7.2 3.2 stack.2
  10.4 8.5 %all-to-all-start = ((bf16[8,4,4,8,1536]{4,3,2,1,0:T(8,128)(2,1)}), bf16[8,4,4,8,1536]{4,3,2,1,0:T(8,128)(2,1)}, u32[]{:S(2)}, u32[]{:S(2)}) async-start(bf16[8,4,4,8,1536]{4,3,2,1,0:T(8,128)(2,1)} %stack.2), calls=%async_computation | async-start | bytes 6291456 | tf_op jit(solution)/shard_map/all_to_all | solution.py:15
  19.5 61.5 %all_gather.15 = bf16[4,40,1536]{2,0,1:T(4,128)(2,1)S(1)} all-gather(bf16[4,5,1536]{2,0,1:T(4,128)(2,1)S(1)} %copy-done.5), channel_id=1, replica_groups=mesh['req'=4,'head'=8,'blk'=4] {'head'}, dimensions={1}, use_global_device_ids=true | all-gather | bytes 552960 | tf_op jit(solution)/shard_map/all_gather | solution.py:109
  86.1 2.4 bitcast_reduce_fusion
  88.7 2.9 fusion.10
  91.7 2.9 fusion.8
  99.0 3.1 copy.97
  111.0 2.1 copy.99
  113.0 3.0 pad_maximum_fusion
  120.4 27.2 %all-gather.4.cloned.1.call-done = bf16[4,1184,3,64]{3,0,2,1:T(4,128)(2,1)} async-done(((bf16[4,296,3,64]{3,0,2,1:T(4,128)(2,1)}), bf16[4,1184,3,64]{3,0,2,1:T(4,128)(2,1)}) %all-gather.4.cloned.1.call-update) | async-done | bytes 1818640 | tf_op jit(solution)/shard_map/all_gather | solution.py:126
  147.6 10.5 %fusion = (f32[4,3,296]{2,1,0:T(4,128)S(1)}, f32[4,3,296,1184]{3,2,1,0:T(8,128)}) fusion(f32[4,1184]{1,0:T(4,128)S(1)} %or_convert_fusion, bf16[4,1184,3,64]{3,0,2,1:T(4,128)(2,1)} %all-gather.4.cloned.1.call-done, bf16[4,40,3,64]{1,3,2,0:T(8,128)(2,1)S(1)} %multiply_convert_fusion.3, bf16[4,256,3,64]{1,3,2,0:T(8,128)(2,1)} %multiply_convert_fusion.1), kind=kOutput, calls=%fused_computation.2 | convolution fusion | flops 551835136 | bytes 19128704 | tf_op jit(solution)/shard_map/rqhd,rkhd->rhqk/dot_general | solution.py:137
  158.1 34.0 %all-gather.6.cloned.1.call-done = bf16[4,1184,3,64]{3,0,2,1:T(4,128)(2,1)} async-done(((bf16[4,296,3,64]{3,0,2,1:T(4,128)(2,1)}), bf16[4,1184,3,64]{3,0,2,1:T(4,128)(2,1)}) %all-gather.6.cloned.1.call-update) | async-done | bytes 1818640 | tf_op jit(solution)/shard_map/all_gather | solution.py:127
  192.1 9.1 %divide_convert_fusion = bf16[4,296,3,64]{1,3,2,0:T(8,128)(2,1)S(1)} fusion(bf16[4,1184,3,64]{3,0,2,1:T(4,128)(2,1)} %all-gather.6.cloned.1.call-done, f32[4,3,296,1184]{3,2,1,0:T(8,128)} %get-tuple-element.49, f32[4,1184]{1,0:T(4,128)S(1)} %or_convert_fusion, f32[4,296,3]{1,2,0:T(4,128)S(1)} %bitcast.226), kind=kOutput, calls=%fused_computation.56 | convolution fusion | flops 547178496 | bytes 19128704 | tf_op jit(solution)/shard_map/rhqk,rkhd->rhqd/dot_general | solution.py:142
  201.2 2.7 fusion.14
  206.7 164.2 %all-reduce.11.cloned.1.call-done = (bf16[4,32,8,1536]{3,2,1,0:T(8,128)(2,1)}, bf16[4,40,1536]{2,0,1:T(4,128)(2,1)}) async-done(((bf16[4,32,8,1536]{3,2,1,0:T(8,128)(2,1)}, bf16[4,40,1536]{2,0,1:T(4,128)(2,1)}), (bf16[4,32,8,1536]{3,2,1,0:T(8,128)(2,1)}, bf16[4,40,1536]{2,0,1:T(4,128)(2,1)})) %all-reduce.11.cloned.1.call-update) | async-done | bytes 3637264
  379.3 30.7 %all_gather.19 = bf16[4,40,1536]{2,0,1:T(4,128)(2,1)S(1)} all-gather(bf16[4,5,1536]{2,0,1:T(4,128)(2,1)S(1)} %add_convert_fusion.5), channel_id=1, replica_groups=mesh['req'=4,'head'=8,'blk'=4] {'head'}, dimensions={1}, use_global_device_ids=true | all-gather | bytes 552960 | tf_op jit(solution)/shard_map/all_gather | solution.py:175
  410.0 4.8 convolution_convert_fusion.2
  416.8 23.0 %all-gather.8.cloned.1.call-done = bf16[4,32,8,1536]{3,2,1,0:T(8,128)(2,1)} async-done(((bf16[4,4,8,1536]{3,2,1,0:T(8,128)(2,1)}), bf16[4,32,8,1536]{3,2,1,0:T(8,128)(2,1)}) %all-gather.8.cloned.1.call-update) | async-done | bytes 3145744 | tf_op jit(solution)/shard_map/all_gather | solution.py:174
  439.8 10.5 %fusion.13 = bf16[4,32,8,1536]{3,2,1,0:T(8,128)(2,1)} fusion(bf16[768,1536]{1,0:T(8,128)(2,1)S(1)} %copy-done, bf16[1536,768]{1,0:T(8,128)(2,1)} %param.34, bf16[4,32,8,1536]{3,2,1,0:T(8,128)(2,1)} %all-gather.8.cloned.1.call-done), kind=kOutput, calls=%fused_computation.20 | convolution fusion | flops 4840488960 | bytes 11010048 | tf_op jit(solution)/shard_map/rnf,fd->rnd/dot_general | solution.py:186
  451.2 161.8 %all-reduce.9.cloned.1.call-done = (bf16[4,32,8,1536]{3,2,1,0:T(8,128)(2,1)}, bf16[4,40,1536]{2,0,1:T(4,128)(2,1)}) async-done(((bf16[4,32,8,1536]{3,2,1,0:T(8,128)(2,1)}, bf16[4,40,1536]{2,0,1:T(4,128)(2,1)}), (bf16[4,32,8,1536]{3,2,1,0:T(8,128)(2,1)}, bf16[4,40,1536]{2,0,1:T(4,128)(2,1)})) %all-reduce.9.cloned.1.call-update) | async-done | bytes 3637264
  614.4 2.2 multiply_reduce_fusion
  624.5 2.8 collective-permute-done.1
  627.4 5.1 collective-permute-start.2
  635.0 2.6 collective-permute-done.3
  (162 shorter events, 50.4 us)
Async XLA Ops:
  7.2 432.7 %copy-start = (bf16[768,1536]{1,0:T(8,128)(2,1)S(1)}, bf16[768,1536]{1,0:T(8,128)(2,1)}, u32[]{:S(2)}) copy-start(bf16[768,1536]{1,0:T(8,128)(2,1)} %param.36) | copy-start | bytes 7077892
  10.4 9.2 %copy-start.5 = (bf16[4,5,1536]{2,0,1:T(4,128)(2,1)S(1)}, bf16[4,5,1536]{2,0,1:T(4,128)(2,1)}, u32[]{:S(2)}) copy-start(bf16[4,5,1536]{2,0,1:T(4,128)(2,1)} %param.21) | copy-start | bytes 184324
  10.4 70.7 %copy-start.14 = (f32[4,6,1536]{2,0,1:T(4,128)S(1)}, f32[4,6,1536]{2,0,1:T(4,128)}, u32[]{:S(2)}) copy-start(f32[4,6,1536]{2,0,1:T(4,128)} %param.26) | copy-start | bytes 442372
  10.4 75.7 %all-to-all-start = ((bf16[8,4,4,8,1536]{4,3,2,1,0:T(8,128)(2,1)}), bf16[8,4,4,8,1536]{4,3,2,1,0:T(8,128)(2,1)}, u32[]{:S(2)}, u32[]{:S(2)}) async-start(bf16[8,4,4,8,1536]{4,3,2,1,0:T(8,128)(2,1)} %stack.2), calls=%async_computation | async-start | bytes 6291456 | tf_op jit(solution)/shard_map/all_to_all | solution.py:15
  18.8 128.8 %all-gather.4.cloned.1.call-start = ((), (), s32[]{:S(2)}) async-start(), calls=%async_computation.1 | async-start | bytes 4546560 | tf_op jit(solution)/shard_map/all_gather | solution.py:126
  18.9 64.8 %copy-start.2 = (bf16[1536,3,192]{0,2,1:T(8,128)(2,1)S(1)}, bf16[1536,3,192]{0,2,1:T(8,128)(2,1)}, u32[]{:S(2)}) copy-start(bf16[1536,3,192]{0,2,1:T(8,128)(2,1)} %param.31) | copy-start | bytes 5308420
  102.2 89.9 %all-gather.6.cloned.1.call-start = ((), (), s32[]{:S(2)}) async-start(), calls=%async_computation.2 | async-start | bytes 4546560 | tf_op jit(solution)/shard_map/all_gather | solution.py:127
  108.4 11.0 %copy-start.25 = (s32[4]{0:T(128)S(1)}, s32[4]{0:T(128)}, u32[]{:S(2)}) copy-start(s32[4]{0:T(128)} %param.23) | copy-start | bytes 52
  116.0 254.9 %all-reduce.11.cloned.1.call-start = ((), (), s32[]{:S(2)}) async-start(), calls=%async_computation.5 | async-start | bytes 7274496
  203.9 167.0 %copy-start.1 = (bf16[4,4,8,1536]{3,2,1,0:T(8,128)(2,1)S(1)}, bf16[4,4,8,1536]{3,2,1,0:T(8,128)(2,1)}, u32[]{:S(2)}) copy-start(bf16[4,4,8,1536]{3,2,1,0:T(8,128)(2,1)} %param.20) | copy-start | bytes 1179652
  203.9 167.0 %copy-start.6 = (f32[4,1536]{1,0:T(4,128)S(1)}, f32[4,1536]{1,0:T(4,128)}, u32[]{:S(2)}) copy-start(f32[4,1536]{1,0:T(4,128)} %get-tuple-element.38) | copy-start | bytes 73732
  204.3 169.2 %copy-start.21 = (f32[4,1536]{1,0:T(4,128)S(1)}, f32[4,1536]{1,0:T(4,128)}, u32[]{:S(2)}) copy-start(f32[4,1536]{1,0:T(4,128)} %get-tuple-element.39) | copy-start | bytes 73732
  205.3 170.9 %copy-start.19 = (f32[4,1,1536]{2,0,1:T(4,128)S(1)}, f32[4,1,1536]{2,0,1:T(4,128)}, u32[]{:S(2)}) copy-start(f32[4,1,1536]{2,0,1:T(4,128)} %get-tuple-element.32) | copy-start | bytes 73732
  205.3 171.0 %copy-start.7 = (f32[4,1536]{1,0:T(4,128)S(1)}, f32[4,1536]{1,0:T(4,128)}, u32[]{:S(2)}) copy-start(f32[4,1536]{1,0:T(4,128)} %get-tuple-element.30) | copy-start | bytes 73732
  205.3 173.0 %copy-start.18 = (f32[4,1536]{1,0:T(4,128)S(1)}, f32[4,1536]{1,0:T(4,128)}, u32[]{:S(2)}) copy-start(f32[4,1536]{1,0:T(4,128)} %get-tuple-element.33) | copy-start | bytes 73732
  205.4 234.5 %all-gather.8.cloned.1.call-start = ((), (), s32[]{:S(2)}) async-start(), calls=%async_computation.3 | async-start | bytes 3538944 | tf_op jit(solution)/shard_map/all_gather | solution.py:174
  375.6 237.4 %all-reduce.9.cloned.1.call-start = ((), (), s32[]{:S(2)}) async-start(), calls=%async_computation.4 | async-start | bytes 7274496
  450.3 162.7 %copy-start.11 = (f32[4,1536]{1,0:T(4,128)S(1)}, f32[4,1536]{1,0:T(4,128)}, u32[]{:S(2)}) copy-start(f32[4,1536]{1,0:T(4,128)} %get-tuple-element.34) | copy-start | bytes 73732
  451.1 167.4 %copy-start.10 = (f32[4,8,16,16]{3,2,1,0:T(8,128)S(1)}, f32[4,8,16,16]{3,2,1,0:T(8,128)}, u32[]{:S(2)}) copy-start(f32[4,8,16,16]{3,2,1,0:T(8,128)} %param.22) | copy-start | bytes 98308
  614.4 9.9 %copy-start.12 = (bf16[3,3,16,512]{3,2,1,0:T(8,128)(2,1)S(1)}, bf16[3,3,16,512]{3,2,1,0:T(8,128)(2,1)}, u32[]{:S(2)}) copy-start(bf16[3,3,16,512]{3,2,1,0:T(8,128)(2,1)} %param.39) | copy-start | bytes 442372
  619.4 5.1 collective-permute-start
  621.4 6.0 collective-permute-start.1
  627.4 7.6 %collective-permute-start.2 = (bf16[4,10,1,16]{3,2,1,0:T(2,128)(2,1)S(1)}, bf16[4,10,1,16]{3,2,1,0:T(2,128)(2,1)S(1)}, u32[]{:S(2)}, u32[]{:S(2)}) collective-permute-start(bf16[4,10,1,16]{3,2,1,0:T(2,128)(2,1)S(1)} %get-tuple-element.26), channel_id=1, source_target_pairs={{0,1},{1,2},{2,3},{4,5},{5,6},{6,7},{8,9},{9,10},{10,11},{12,13},{... | collective-permute-start | bytes 3848 | tf_op jit(solution)/shard_map/ppermute | solution.py:28
  632.5 5.1 collective-permute-start.3
  (15 other events, 55.2 us)
Sparse Core Ops, SparseCore 0:
  102.3 45.3 all-gather.3
  149.3 42.7 all-gather.5
  205.5 165.4 all-reduce.10
  375.7 64.0 all-gather.7
  450.4 162.4 all-reduce.8
